TPU v7x, 32 devices: a whole 2x2x4 slice. The times are simulated.
32 devices in a mesh: dp: 4 (over y, x), seq: 8 (over z, core).
Axes of the slice: x: 2, y: 2, z: 4, core: 2. Of those that a mesh axis runs over, the one named last changes fastest.
Arguments:
- queries: bfloat16 [4, 8, 512, 2048], P('dp', 'seq'), may hold values from -48 to 48
- keys: bfloat16 [4, 8, 512, 2048], P('dp', 'seq'), may hold values from -6 to 6
- values: bfloat16 [4, 8, 512, 2048], P('dp', 'seq'), may hold values from -6 to 6
- out_grad: bfloat16 [4, 8, 512, 2048], P('dp', 'seq'), may hold values from -6 to 6
- out_weight: bfloat16 [2048, 2048], P('dp'), may hold values from -0.125 to 0.125
- row_mask: int32 [4, 4], replicated, may hold values from 0 to 1, as said below
- col_mask: int32 [8, 8], replicated, may hold values from 0 to 1, as said below
Outputs:
- layer_out: bfloat16 [4, 8, 512, 2048], P('dp', 'seq')
- query_grad: bfloat16 [4, 8, 512, 2048], P('dp', 'seq')
- key_grad: bfloat16 [4, 8, 512, 2048], P('dp', 'seq')
- value_grad: bfloat16 [4, 8, 512, 2048], P('dp', 'seq')
- wo_grad: float32 [2048, 2048], P(('dp', 'seq'))
Inputs may be any that keep to these rules, and one draw needn't show every extreme that they name: row_mask[a, b] is 1 for b = a and 0 for b > a. col_mask[r, s] is 1 for s = r and for s = r - 1, and 0 for s > r.
All inputs are finite; a program needn't handle non-finite values.
Results may differ from a plain program's by a relative error of at most 0.012.
Values may be sent and summed in bfloat16 or wider, within the bound.
No kernel may reach another device: no remote copies, remote signals or barrier semaphores. Data moves between devices by JAX's collectives and lax.ppermute only.
A program may use at most 192 MiB of HBM per device.

v0:
```python
import math
import jax
import jax.numpy as jnp
from jax import lax
from jax.sharding import PartitionSpec as P

DH = 128
COLS = 512
BLK = 128
masked_out = -1e30
scale = 1.0 / math.sqrt(DH)


def row_permit(row_mask):
    spread = jnp.repeat(jnp.repeat(row_mask, BLK, axis=0), BLK, axis=1)
    row_index = lax.broadcasted_iota(jnp.int32, (COLS, COLS), 0)
    col_index = lax.broadcasted_iota(jnp.int32, (COLS, COLS), 1)
    return (spread == 1) & (col_index <= row_index)


def softmax_parts(scores, allowed):
    highest = jnp.max(jnp.where(allowed, scores, masked_out), axis=-1, keepdims=True)
    attend = jnp.exp(jnp.where(allowed, scores - highest, masked_out))
    totals = jnp.sum(attend, axis=-1, keepdims=True)
    probs = (attend / totals).astype(jnp.bfloat16)
    return (probs, highest + jnp.log(totals))


def row_forward(q, k, v, allowed):
    scores = jnp.einsum("ihd,jhd->hij", q, k, preferred_element_type=jnp.float32) * scale
    probs, log_total = softmax_parts(scores, allowed[None])
    out = jnp.einsum("hij,jhd->ihd", probs, v, preferred_element_type=jnp.float32)
    return (out.astype(jnp.bfloat16), scores, log_total)


def row_backward(q, k, v, out, grad, scores, log_total, allowed):
    grad_dot = jnp.einsum("ihd,ihd->hi", grad, out, preferred_element_type=jnp.float32)
    back = jnp.where(allowed[None], jnp.exp(scores - log_total), 0.0)
    value_grad = jnp.einsum(
        "hij,ihd->jhd", back.astype(jnp.bfloat16), grad, preferred_element_type=jnp.float32
    )
    prob_grad = jnp.einsum("ihd,jhd->hij", grad, v, preferred_element_type=jnp.float32)
    score_grad = (back * (prob_grad - grad_dot[..., None])).astype(jnp.bfloat16)
    query_grad = jnp.einsum("hij,jhd->ihd", score_grad, k, preferred_element_type=jnp.float32)
    key_grad = jnp.einsum("hij,ihd->jhd", score_grad, q, preferred_element_type=jnp.float32)
    return tuple(
        (g.astype(jnp.bfloat16) for g in (query_grad * scale, key_grad * scale, value_grad))
    )


def column_forward(q, k, v, allowed):
    scores = jnp.einsum("rchd,schd->chrs", q, k, preferred_element_type=jnp.float32) * scale
    probs, log_total = softmax_parts(scores, allowed)
    out = jnp.einsum("chrs,schd->rchd", probs, v, preferred_element_type=jnp.float32)
    return (out.astype(jnp.bfloat16), scores, log_total)


def column_backward(q, k, v, out, grad, scores, log_total, allowed):
    grad_dot = jnp.einsum("rchd,rchd->chr", grad, out, preferred_element_type=jnp.float32)
    back = jnp.where(allowed, jnp.exp(scores - log_total), 0.0)
    value_grad = jnp.einsum(
        "chrs,rchd->schd", back.astype(jnp.bfloat16), grad, preferred_element_type=jnp.float32
    )
    prob_grad = jnp.einsum("rchd,schd->chrs", grad, v, preferred_element_type=jnp.float32)
    score_grad = (back * (prob_grad - grad_dot[..., None])).astype(jnp.bfloat16)
    query_grad = jnp.einsum("chrs,schd->rchd", score_grad, k, preferred_element_type=jnp.float32)
    key_grad = jnp.einsum("chrs,rchd->schd", score_grad, q, preferred_element_type=jnp.float32)
    return tuple(
        (g.astype(jnp.bfloat16) for g in (query_grad * scale, key_grad * scale, value_grad))
    )


def on_device(queries, keys, values, out_grad, out_weight, row_mask, col_mask):
    tokens, features = (queries.shape[2], queries.shape[3])
    half = features // 2
    heads_half = half // DH
    rows = lax.axis_size("seq")
    cols_each = tokens // rows
    weight = lax.all_gather(out_weight, "dp", axis=0, tiled=True)
    chunks = 2
    piece = cols_each // chunks

    def chunked(t):
        return t.reshape(rows, chunks, piece, half).transpose(1, 0, 2, 3)

    packed = jnp.stack([chunked(t[0, 0, :, half:]) for t in (queries, keys, values)], axis=1)
    col_ok = col_mask == 1
    shipped_all = [
        lax.all_to_all(packed[j], "seq", split_axis=1, concat_axis=1, tiled=True)
        for j in range(chunks)
    ]
    row_ok = row_permit(row_mask)
    split = lambda t: t[0, 0, :, :half].reshape(tokens, heads_half, DH)
    row_q, row_k, row_v = (split(queries), split(keys), split(values))
    row_out, row_scores, row_total = row_forward(row_q, row_k, row_v, row_ok)
    row_attn = row_out.reshape(tokens, half)
    flat_grad = out_grad[0, 0]
    contract = (((0,), (0,)), ((), ()))
    row_done, shipped_first = lax.optimization_barrier(
        ((row_out, row_scores, row_total), shipped_all[0])
    )
    row_out, row_scores, row_total = row_done
    row_attn = row_out.reshape(tokens, half)
    shipped_all[0] = shipped_first
    col_state = []
    col_back = []
    for j in range(chunks):
        shipped = shipped_all[j]
        col_q, col_k, col_v = (shipped[i].reshape(rows, piece, heads_half, DH) for i in range(3))
        col_out, col_scores, col_total = column_forward(col_q, col_k, col_v, col_ok)
        col_state.append((col_q, col_k, col_v, col_out, col_scores, col_total))
        col_back.append(col_out.reshape(rows, piece, half))
    col_attn = lax.all_to_all(
        jnp.stack(col_back, axis=1), "seq", split_axis=0, concat_axis=0, tiled=True
    ).reshape(tokens, half)
    attention = jnp.concatenate([row_attn, col_attn], axis=1)
    partial = lax.dot_general(attention, flat_grad, contract, preferred_element_type=jnp.float32)
    by_rows_of = (((1,), (1,)), ((), ()))
    row_grad = lax.dot_general(
        flat_grad, weight[:half], by_rows_of, preferred_element_type=jnp.float32
    ).astype(jnp.bfloat16)
    partial, late_weight = lax.optimization_barrier((partial, weight))
    col_grad = lax.dot_general(
        flat_grad, late_weight[half:], by_rows_of, preferred_element_type=jnp.float32
    ).astype(jnp.bfloat16)
    grad_col_part = chunked(col_grad)
    devices_all = lax.axis_size(("dp", "seq"))
    wo_grad = lax.psum_scatter(
        partial.astype(jnp.bfloat16), ("dp", "seq"), scatter_dimension=0, tiled=True
    ).astype(jnp.float32) * (1.0 / math.sqrt(tokens * devices_all))
    col_grads_back = []
    for j in range(chunks):
        grad_cols = lax.all_to_all(
            grad_col_part[j], "seq", split_axis=0, concat_axis=0, tiled=True
        ).reshape(rows, piece, heads_half, DH)
        col_q, col_k, col_v, col_out, col_scores, col_total = col_state[j]
        col_grads = column_backward(
            col_q, col_k, col_v, col_out, grad_cols, col_scores, col_total, col_ok
        )
        col_grads_back.append(
            lax.all_to_all(
                jnp.stack([g.reshape(rows, piece, half) for g in col_grads]),
                "seq",
                split_axis=1,
                concat_axis=1,
                tiled=True,
            )
        )
    col_grads_whole = jnp.stack(col_grads_back, axis=2).reshape(3, tokens, half)
    row_grads = row_backward(
        row_q,
        row_k,
        row_v,
        row_out,
        row_grad.reshape(tokens, heads_half, DH),
        row_scores,
        row_total,
        row_ok,
    )
    layer_out = jnp.dot(attention, weight, preferred_element_type=jnp.float32).astype(jnp.bfloat16)
    grads = [
        jnp.concatenate([row_grads[i].reshape(tokens, half), col_grads_whole[i]], axis=1)[
            None, None
        ]
        for i in range(3)
    ]
    return (layer_out[None, None], grads[0], grads[1], grads[2], wo_grad)


def solution(mesh):
    in_specs = (
        P("dp", "seq", None, None),
        P("dp", "seq", None, None),
        P("dp", "seq", None, None),
        P("dp", "seq", None, None),
        P("dp", None),
        P(),
        P(),
    )
    out_specs = (
        P("dp", "seq", None, None),
        P("dp", "seq", None, None),
        P("dp", "seq", None, None),
        P("dp", "seq", None, None),
        P(("dp", "seq"), None),
    )
    return jax.shard_map(
        on_device, mesh=mesh, in_specs=in_specs, out_specs=out_specs, check_vma=False
    )
```

profile of v0, /device:TPU:0, one launch (start us, length us, event | category | flops | bytes accessed | tf_op | source)
XLA Modules:
  0.0 367.7 jit_solution(15175648478473161992)
XLA Ops:
  15.7 6.3 %all-to-all-start.1 = ((bf16[3,8,32,1024]{3,2,0,1:T(8,128)(2,1)}), bf16[3,8,32,1024]{3,2,0,1:T(8,128)(2,1)}, u32[]{:S(2)}, u32[]{:S(2)}) async-start(bf16[3,8,32,1024]{3,2,0,1:T(8,128)(2,1)} %copy.219), calls=%async_computation.1 | async-start | bytes 3145728 | tf_op jit(solution)/shard_map/all_to_all | solution.py:89
  30.7 29.2 %all-to-all-done.1 = bf16[3,8,32,1024]{3,2,0,1:T(8,128)(2,1)} async-done(((bf16[3,8,32,1024]{3,2,0,1:T(8,128)(2,1)}), bf16[3,8,32,1024]{3,2,0,1:T(8,128)(2,1)}, u32[]{:S(2)}, u32[]{:S(2)}) %all-to-all-start.1) | async-done | bytes 1572896 | tf_op jit(solution)/shard_map/all_to_all | solution.py:89
  59.9 4.6 %all-to-all-start = ((bf16[3,8,32,1024]{3,2,0,1:T(8,128)(2,1)}), bf16[3,8,32,1024]{3,2,0,1:T(8,128)(2,1)}, u32[]{:S(2)}, u32[]{:S(2)}) async-start(bf16[3,8,32,1024]{3,2,0,1:T(8,128)(2,1)} %copy.211), calls=%async_computation | async-start | bytes 3145728 | tf_op jit(solution)/shard_map/all_to_all | solution.py:89
  64.5 2.9 select_reduce_fusion
  70.7 3.6 fusion.36
  78.5 23.8 %all-to-all-done = bf16[3,8,32,1024]{3,2,0,1:T(8,128)(2,1)} async-done(((bf16[3,8,32,1024]{3,2,0,1:T(8,128)(2,1)}), bf16[3,8,32,1024]{3,2,0,1:T(8,128)(2,1)}, u32[]{:S(2)}, u32[]{:S(2)}) %all-to-all-start) | async-done | bytes 1572896 | tf_op jit(solution)/shard_map/all_to_all | solution.py:89
  121.2 4.2 %all-to-all-start.2 = ((bf16[8,2,32,1024]{3,2,1,0:T(8,128)(2,1)}), bf16[8,2,32,1024]{3,2,1,0:T(8,128)(2,1)}, u32[]{:S(2)}, u32[]{:S(2)}) async-start(bf16[8,2,32,1024]{3,2,1,0:T(8,128)(2,1)} %copy.225), calls=%async_computation.2 | async-start | bytes 2097152 | tf_op jit(solution)/shard_map/all_to_all | solution.py:113
  128.3 23.7 %all-to-all-done.2 = bf16[8,2,32,1024]{3,2,1,0:T(8,128)(2,1)} async-done(((bf16[8,2,32,1024]{3,2,1,0:T(8,128)(2,1)}), bf16[8,2,32,1024]{3,2,1,0:T(8,128)(2,1)}, u32[]{:S(2)}, u32[]{:S(2)}) %all-to-all-start.2) | async-done | bytes 1048608 | tf_op jit(solution)/shard_map/all_to_all | solution.py:113
  154.3 8.3 %fusion.14 = bf16[2048,2048]{1,0:T(8,128)(2,1)} fusion(bf16[1,1,512,2048]{3,2,1,0:T(8,128)(2,1)S(1)} %copy-done, bf16[512,1024]{0,1:T(8,128)(2,1)} %copy.226, bf16[512,1024]{0,1:T(8,128)(2,1)} %bitcast.241), kind=kOutput, calls=%fused_computation.29 | convolution fusion | flops 4299161600 | bytes 12582912 | tf_op jit(solution)/shard_map/dot_general | solution.py:117
  162.6 4.5 %fusion.18 = bf16[1024,512]{0,1:T(8,128)(2,1)S(1)} fusion(bf16[1,1,512,2048]{3,2,1,0:T(8,128)(2,1)S(1)} %copy-done, bf16[2048,2048]{1,0:T(8,128)(2,1)} %all-gather.2.cloned.1.call-done), kind=kOutput, calls=%fused_computation.42 | convolution fusion | flops 2148007936 | bytes 7340032 | tf_op jit(solution)/shard_map/dot_general | solution.py:123
  168.4 4.2 %all-to-all-start.3 = ((bf16[8,32,1024]{2,1,0:T(8,128)(2,1)}), bf16[8,32,1024]{2,1,0:T(8,128)(2,1)}, u32[]{:S(2)}, u32[]{:S(2)}) async-start(bf16[8,32,1024]{2,1,0:T(8,128)(2,1)} %get-tuple-element.37), calls=%async_computation.3 | async-start | bytes 1048576 | tf_op jit(solution)/shard_map/all_to_all | solution.py:133
  174.3 20.8 %all-to-all-done.3 = bf16[8,32,1024]{2,1,0:T(8,128)(2,1)} async-done(((bf16[8,32,1024]{2,1,0:T(8,128)(2,1)}), bf16[8,32,1024]{2,1,0:T(8,128)(2,1)}, u32[]{:S(2)}, u32[]{:S(2)}) %all-to-all-start.3) | async-done | bytes 524320 | tf_op jit(solution)/shard_map/all_to_all | solution.py:133
  195.1 4.2 %all-to-all-start.5 = ((bf16[8,32,1024]{2,1,0:T(8,128)(2,1)}), bf16[8,32,1024]{2,1,0:T(8,128)(2,1)}, u32[]{:S(2)}, u32[]{:S(2)}) async-start(bf16[8,32,1024]{2,1,0:T(8,128)(2,1)} %get-tuple-element.36), calls=%async_computation.5 | async-start | bytes 1048576 | tf_op jit(solution)/shard_map/all_to_all | solution.py:133
  223.0 4.5 %all-to-all-start.4 = ((bf16[3,8,32,1024]{3,2,0,1:T(8,128)(2,1)}), bf16[3,8,32,1024]{3,2,0,1:T(8,128)(2,1)}, u32[]{:S(2)}, u32[]{:S(2)}) async-start(bf16[3,8,32,1024]{3,2,0,1:T(8,128)(2,1)} %copy.242), calls=%async_computation.4 | async-start | bytes 3145728 | tf_op jit(solution)/shard_map/all_to_all | solution.py:141
  227.5 4.6 %fusion.31 = bf16[64,8,8,128]{3,1,2,0:T(8,128)(2,1)S(1)} fusion(bf16[2048,2048]{1,0:T(8,128)(2,1)} %all-gather.2.cloned.1.call-done, bf16[1,1,512,2048]{3,2,1,0:T(8,128)(2,1)S(1)} %copy-done), kind=kOutput, calls=%fused_computation.45 | convolution fusion | flops 2148007936 | bytes 7340032 | tf_op jit(solution)/shard_map/dot_general | solution.py:119
  256.5 26.0 %all-to-all-done.4 = bf16[3,8,32,1024]{3,2,0,1:T(8,128)(2,1)} async-done(((bf16[3,8,32,1024]{3,2,0,1:T(8,128)(2,1)}), bf16[3,8,32,1024]{3,2,0,1:T(8,128)(2,1)}, u32[]{:S(2)}, u32[]{:S(2)}) %all-to-all-start.4) | async-done | bytes 1572896 | tf_op jit(solution)/shard_map/all_to_all | solution.py:141
  282.4 5.8 %all-to-all-start.6 = ((bf16[3,8,32,1024]{3,2,0,1:T(8,128)(2,1)}), bf16[3,8,32,1024]{3,2,0,1:T(8,128)(2,1)}, u32[]{:S(2)}, u32[]{:S(2)}) async-start(bf16[3,8,32,1024]{3,2,0,1:T(8,128)(2,1)} %copy.254), calls=%async_computation.6 | async-start | bytes 3145728 | tf_op jit(solution)/shard_map/all_to_all | solution.py:141
  288.3 5.5 %multiply_convert_fusion = bf16[8,512,512]{1,2,0:T(8,128)(2,1)S(1)} fusion(f32[8,512,512]{1,2,0:T(8,128)} %copy-done.1, f32[8,512]{1,0:T(8,128)S(1)} %multiply_reduce_fusion, f32[8,512]{1,0:T(8,128)S(1)} %bitcast.246, pred[512,512]{0,1:T(8,128)(4,1)S(1)} %fusion.53, bf16[512,8,128]{0,2,1:T(8,128)(2,1)} %copy.259, bf16[512,8,128]{0,2,1:T(8,128)(2,1)S(1)} %bitcast.214), kind=kOutput, calls=%fused_computation | convolution fusion | flops 547356672 | bytes 14974976 | tf_op jit(solution)/shard_map/ihd,jhd->hij/dot_general | solution.py:42
  297.2 5.1 %multiply_convert_fusion.1 = bf16[8,512,128]{1,2,0:T(8,128)(2,1)} fusion(bf16[8,512,512]{1,2,0:T(8,128)(2,1)} %copy-done.2, bf16[512,8,128]{0,2,1:T(8,128)(2,1)} %bitcast.224), kind=kOutput, calls=%fused_computation.33 | convolution fusion | flops 537919488 | bytes 6291456 | tf_op jit(solution)/shard_map/hij,ihd->jhd/dot_general | solution.py:45
  304.6 6.0 %fusion.28 = bf16[8,128,512]{2,1,0:T(8,128)(2,1)} fusion(bf16[512,8,128]{0,2,1:T(8,128)(2,1)S(1)} %copy-done.20, f32[8,512,512]{1,2,0:T(8,128)} %copy-done.1, f32[8,512]{1,0:T(8,128)S(1)} %bitcast.247, pred[512,512]{0,1:T(8,128)(4,1)S(1)} %fusion.53), kind=kOutput, calls=%fused_computation.44 | convolution fusion | flops 543686656 | bytes 10764288 | tf_op jit(solution)/shard_map/hij,ihd->jhd/dot_general | solution.py:39
  312.1 10.0 %fusion.12 = bf16[1,1,512,2048]{3,2,1,0:T(8,128)(2,1)} fusion(bf16[2048,2048]{1,0:T(8,128)(2,1)} %all-gather.2.cloned.1.call-done, bf16[512,1024]{0,1:T(8,128)(2,1)} %copy.226, bf16[512,1024]{0,1:T(8,128)(2,1)} %bitcast.242), kind=kOutput, calls=%fused_computation.23 | convolution fusion | flops 4300210176 | bytes 12582912 | tf_op jit(solution)/shard_map/dot_general | solution.py:160
  322.0 2.8 copy.356
  324.8 19.7 %all-to-all-done.6 = bf16[3,8,32,1024]{3,2,0,1:T(8,128)(2,1)} async-done(((bf16[3,8,32,1024]{3,2,0,1:T(8,128)(2,1)}), bf16[3,8,32,1024]{3,2,0,1:T(8,128)(2,1)}, u32[]{:S(2)}, u32[]{:S(2)}) %all-to-all-start.6) | async-done | bytes 1572896 | tf_op jit(solution)/shard_map/all_to_all | solution.py:141
  351.2 7.6 %reduce-scatter.2.cloned.1.call-done = bf16[64,2048]{1,0:T(8,128)(2,1)} async-done(((bf16[2048,2048]{1,0:T(8,128)(2,1)}), bf16[64,2048]{1,0:T(8,128)(2,1)}) %reduce-scatter.2.cloned.1.call-update) | async-done | bytes 262160 | tf_op jit(solution)/shard_map/reduce_scatter | solution.py:128
  (181 shorter events, 114.9 us)
Async XLA Ops:
  7.2 147.1 %copy-start = (bf16[1,1,512,2048]{3,2,1,0:T(8,128)(2,1)S(1)}, bf16[1,1,512,2048]{3,2,1,0:T(8,128)(2,1)}, u32[]{:S(2)}) copy-start(bf16[1,1,512,2048]{3,2,1,0:T(8,128)(2,1)} %param.10) | copy-start | bytes 6291460
  7.2 155.4 %all-gather.2.cloned.1.call-start = ((), (), s32[]{:S(2)}) async-start(), calls=%async_computation.8 | async-start | bytes 10485760 | tf_op jit(solution)/shard_map/all_gather | solution.py:79
  14.3 7.6 %copy-start.43 = (s32[4,4]{1,0:T(4,128)S(1)}, s32[4,4]{1,0:T(4,128)}, u32[]{:S(2)}) copy-start(s32[4,4]{1,0:T(4,128)} %param.12) | copy-start | bytes 196
  14.4 7.8 %copy-start.42 = (s32[8,8]{1,0:T(8,128)S(1)}, s32[8,8]{1,0:T(8,128)}, u32[]{:S(2)}) copy-start(s32[8,8]{1,0:T(8,128)} %param.13) | copy-start | bytes 772
  15.7 44.3 %all-to-all-start.1 = ((bf16[3,8,32,1024]{3,2,0,1:T(8,128)(2,1)}), bf16[3,8,32,1024]{3,2,0,1:T(8,128)(2,1)}, u32[]{:S(2)}, u32[]{:S(2)}) async-start(bf16[3,8,32,1024]{3,2,0,1:T(8,128)(2,1)} %copy.219), calls=%async_computation.1 | async-start | bytes 3145728 | tf_op jit(solution)/shard_map/all_to_all | solution.py:89
  22.2 186.8 %copy-start.39 = (pred[8,8]{0,1:T(8,128)(4,1)}, pred[8,8]{0,1:T(8,128)(4,1)S(1)}, u32[]{:S(2)}) copy-start(pred[8,8]{0,1:T(8,128)(4,1)S(1)} %copy.213) | copy-start | bytes 196
  25.3 39.2 %copy-start.5 = (bf16[1,1,512,1024]{2,3,1,0:T(8,128)(2,1)}, bf16[1,1,512,1024]{2,3,1,0:T(8,128)(2,1)S(1)}, u32[]{:S(2)}) copy-start(bf16[1,1,512,1024]{2,3,1,0:T(8,128)(2,1)S(1)} %copy.296) | copy-start | bytes 3145732
  59.9 42.4 %all-to-all-start = ((bf16[3,8,32,1024]{3,2,0,1:T(8,128)(2,1)}), bf16[3,8,32,1024]{3,2,0,1:T(8,128)(2,1)}, u32[]{:S(2)}, u32[]{:S(2)}) async-start(bf16[3,8,32,1024]{3,2,0,1:T(8,128)(2,1)} %copy.211), calls=%async_computation | async-start | bytes 3145728 | tf_op jit(solution)/shard_map/all_to_all | solution.py:89
  105.0 3.5 copy-start.31
  105.9 7.0 %copy-start.37 = (f32[32,8,8]{2,1,0:T(8,128)}, f32[32,8,8]{2,1,0:T(8,128)S(1)}, u32[]{:S(2)}) copy-start(f32[32,8,8]{2,1,0:T(8,128)S(1)} %get-tuple-element.40) | copy-start | bytes 24580
  121.2 30.8 %all-to-all-start.2 = ((bf16[8,2,32,1024]{3,2,1,0:T(8,128)(2,1)}), bf16[8,2,32,1024]{3,2,1,0:T(8,128)(2,1)}, u32[]{:S(2)}, u32[]{:S(2)}) async-start(bf16[8,2,32,1024]{3,2,1,0:T(8,128)(2,1)} %copy.225), calls=%async_computation.2 | async-start | bytes 2097152 | tf_op jit(solution)/shard_map/all_to_all | solution.py:113
  125.4 233.4 %reduce-scatter.2.cloned.1.call-start = ((), (), s32[]{:S(2)}) async-start(), calls=%async_computation.9 | async-start | bytes 8650752 | tf_op jit(solution)/shard_map/reduce_scatter | solution.py:128
  168.4 26.7 %all-to-all-start.3 = ((bf16[8,32,1024]{2,1,0:T(8,128)(2,1)}), bf16[8,32,1024]{2,1,0:T(8,128)(2,1)}, u32[]{:S(2)}, u32[]{:S(2)}) async-start(bf16[8,32,1024]{2,1,0:T(8,128)(2,1)} %get-tuple-element.37), calls=%async_computation.3 | async-start | bytes 1048576 | tf_op jit(solution)/shard_map/all_to_all | solution.py:133
  195.1 27.9 %all-to-all-start.5 = ((bf16[8,32,1024]{2,1,0:T(8,128)(2,1)}), bf16[8,32,1024]{2,1,0:T(8,128)(2,1)}, u32[]{:S(2)}, u32[]{:S(2)}) async-start(bf16[8,32,1024]{2,1,0:T(8,128)(2,1)} %get-tuple-element.36), calls=%async_computation.5 | async-start | bytes 1048576 | tf_op jit(solution)/shard_map/all_to_all | solution.py:133
  206.0 4.7 %copy-start.26 = (bf16[32,8,8,128]{3,2,1,0:T(8,128)(2,1)S(1)}, bf16[32,8,8,128]{3,2,1,0:T(8,128)(2,1)}, u32[]{:S(2)}) copy-start(bf16[32,8,8,128]{3,2,1,0:T(8,128)(2,1)} %copy-done.25) | copy-start | bytes 1572868
  223.0 59.4 %all-to-all-start.4 = ((bf16[3,8,32,1024]{3,2,0,1:T(8,128)(2,1)}), bf16[3,8,32,1024]{3,2,0,1:T(8,128)(2,1)}, u32[]{:S(2)}, u32[]{:S(2)}) async-start(bf16[3,8,32,1024]{3,2,0,1:T(8,128)(2,1)} %copy.242), calls=%async_computation.4 | async-start | bytes 3145728 | tf_op jit(solution)/shard_map/all_to_all | solution.py:141
  235.8 4.3 %copy-start.40 = (pred[8,8]{0,1:T(8,128)(4,1)S(1)}, pred[8,8]{0,1:T(8,128)(4,1)}, u32[]{:S(2)}) copy-start(pred[8,8]{0,1:T(8,128)(4,1)} %copy-done.39) | copy-start | bytes 196
  243.7 4.7 %copy-start.17 = (bf16[32,8,8,128]{3,2,1,0:T(8,128)(2,1)S(1)}, bf16[32,8,8,128]{3,2,1,0:T(8,128)(2,1)}, u32[]{:S(2)}) copy-start(bf16[32,8,8,128]{3,2,1,0:T(8,128)(2,1)} %copy.304) | copy-start | bytes 1572868
  248.4 3.5 copy-start.15
  255.1 33.1 %copy-start.19 = (bf16[1,1,512,1024]{2,3,1,0:T(8,128)(2,1)S(1)}, bf16[1,1,512,1024]{2,3,1,0:T(8,128)(2,1)}, u32[]{:S(2)}) copy-start(bf16[1,1,512,1024]{2,3,1,0:T(8,128)(2,1)} %copy.297) | copy-start | bytes 3145732
  255.1 33.1 %copy-start.38 = (f32[8,512,1]{1,0,2:T(8,128)S(1)}, f32[8,512,1]{1,0,2:T(8,128)}, u32[]{:S(2)}) copy-start(f32[8,512,1]{1,0,2:T(8,128)} %add_bitcast_fusion) | copy-start | bytes 49156
  282.4 62.1 %all-to-all-start.6 = ((bf16[3,8,32,1024]{3,2,0,1:T(8,128)(2,1)}), bf16[3,8,32,1024]{3,2,0,1:T(8,128)(2,1)}, u32[]{:S(2)}, u32[]{:S(2)}) async-start(bf16[3,8,32,1024]{3,2,0,1:T(8,128)(2,1)} %copy.254), calls=%async_computation.6 | async-start | bytes 3145728 | tf_op jit(solution)/shard_map/all_to_all | solution.py:141
  288.3 5.6 %copy-start.6 = (bf16[1,1,512,1024]{2,3,1,0:T(8,128)(2,1)S(1)}, bf16[1,1,512,1024]{2,3,1,0:T(8,128)(2,1)}, u32[]{:S(2)}) copy-start(bf16[1,1,512,1024]{2,3,1,0:T(8,128)(2,1)} %copy-done.5) | copy-start | bytes 3145732
  297.2 7.3 %copy-start.20 = (bf16[512,8,128]{0,2,1:T(8,128)(2,1)S(1)}, bf16[512,8,128]{0,2,1:T(8,128)(2,1)}, u32[]{:S(2)}) copy-start(bf16[512,8,128]{0,2,1:T(8,128)(2,1)} %copy.259) | copy-start | bytes 3145732
  (29 other events, 58.2 us)
Sparse Core Ops, SparseCore 0:
  9.9 90.2 all-gather.1
  162.8 196.0 reduce-scatter.1
where the time goes:
time: 372 us; the launch traced here: 368 us
  waiting for transfers between devices  153 us (41%)
  local copies, waits for them, and re-layouts  75.6 us (20%)
  matrix products  65.5 us (18%)
  starting transfers between devices  34.4 us (9%)
  other arithmetic  24.4 us (7%)
  between operations  15 us (4%)
    all_to_all x2, waiting for transfers between devices, on_device(): lax.all_to_all(packed[j], 'seq', split_axis=1, concat_axis=1, tiled=True)  53 us
    all_to_all x2, waiting for transfers between devices, on_device(): lax.all_to_all(jnp.stack([g.reshape(rows, piece, half) for g in col_grads...  45.6 us
    all_to_all x1, waiting for transfers between devices, on_device(): lax.all_to_all(jnp.stack(col_back, axis=1), 'seq', split_axis=0, concat_a...  23.7 us
    all_to_all x2, waiting for transfers between devices, on_device(): lax.all_to_all(grad_col_part[j], 'seq', split_axis=0, concat_axis=0, tile...  22.1 us
    unnamed x102, local copies, waits for them, and re-layouts  20.3 us
    another operation x8, local copies, waits for them, and re-layouts, on_device(): jnp.stack([g.reshape(rows, piece, half) for g in col_grads])  13.2 us
    all_to_all x2, starting transfers between devices, on_device(): lax.all_to_all(packed[j], 'seq', split_axis=1, concat_axis=1, tiled=True)  10.9 us
    all_to_all x2, starting transfers between devices, on_device(): lax.all_to_all(jnp.stack([g.reshape(rows, piece, half) for g in col_grads...  10.3 us
  transfers between devices with their start and end apart: 9, of which 8 were waited for; matrix products, arithmetic and copies ran while one was open for 43% of the time, Pallas kernels for 0%

commit v1 on v0

--- a/solution.py
+++ b/solution.py
@@ -9,6 +9,22 @@
 BLK = 128
 masked_out = -1e30
 scale = 1.0 / math.sqrt(DH)
+
+
+def convert_spot(chunk, pos_dim, block_here):
+    kept_arr = chunk.shape
+    ready = chunk.reshape(
+        *kept_arr[:pos_dim], block_here, kept_arr[pos_dim] // block_here, *kept_arr[pos_dim + 1 :]
+    )
+    k_now = jnp.moveaxis(ready, pos_dim, 0)
+    return k_now
+
+
+def shelves_use(patch, d_out):
+    patch = jnp.moveaxis(patch, 0, d_out)
+    moved = patch.shape
+    aux = patch.reshape(*moved[:d_out], moved[d_out] * moved[d_out + 1], *moved[d_out + 2 :])
+    return aux
 
 
 def row_permit(row_mask):
@@ -130,9 +146,24 @@
     ).astype(jnp.float32) * (1.0 / math.sqrt(tokens * devices_all))
     col_grads_back = []
     for j in range(chunks):
-        grad_cols = lax.all_to_all(
-            grad_col_part[j], "seq", split_axis=0, concat_axis=0, tiled=True
-        ).reshape(rows, piece, heads_half, DH)
+
+        def update_cube(z, chip_axis, m, unit):
+            all_rows = lax.axis_size(chip_axis)
+            x_now = lax.axis_index(chip_axis)
+            reached, r2 = (all_rows, x_now)
+            new = convert_spot(z, m, reached)
+            windows = [new[r2]]
+            for d in range(1, reached):
+                part_now = new[r2 ^ d]
+                work_now = lax.ppermute(
+                    part_now, chip_axis, [(at, at ^ d) for at in range(reached)]
+                )
+                windows.append(work_now)
+            new = jnp.stack(windows, axis=0)[r2 ^ jnp.arange(reached)]
+            step_out = shelves_use(new, unit)
+            return step_out
+
+        grad_cols = update_cube(grad_col_part[j], "seq", 0, 0).reshape(rows, piece, heads_half, DH)
         col_q, col_k, col_v, col_out, col_scores, col_total = col_state[j]
         col_grads = column_backward(
             col_q, col_k, col_v, col_out, grad_cols, col_scores, col_total, col_ok

time: 372 us -> 396 us (1.065)
  waiting for transfers between devices: 153 us -> 180 us
  starting transfers between devices: 34.4 us -> 38.9 us
  other arithmetic: 24.4 us -> 20.1 us
    ppermute x0 -> x14, waiting for transfers between devices: none -> 96.5 us  [update_cube(): lax.ppermute(part_now, chip_axis, [(at, at ^ d) for at in range(reached)])]
    all_to_all x2, waiting for transfers between devices: 45.6 us -> 5.64 us  [on_device(): lax.all_to_all(jnp.stack([g.reshape(rows, piece, half) for g in col_grads...]
    all_to_all x2 -> x0, waiting for transfers between devices: 22.1 us -> none  [on_device(): lax.all_to_all(grad_col_part[j], 'seq', split_axis=0, concat_axis=0, tile...]
    ppermute x0 -> x14, starting transfers between devices: none -> 14.5 us  [update_cube(): lax.ppermute(part_now, chip_axis, [(at, at ^ d) for at in range(reached)])]
    all_to_all x2 -> x0, starting transfers between devices: 8.31 us -> none  [on_device(): lax.all_to_all(grad_col_part[j], 'seq', split_axis=0, concat_axis=0, tile...]
    reduce_scatter x1, waiting for transfers between devices: 7.6 us -> 0.01 us  [on_device(): lax.psum_scatter(partial.astype(jnp.bfloat16), ('dp', 'seq'), scatter_dim...]
    unnamed x102 -> x126, local copies, waits for them, and re-layouts: 20.3 us -> 24.1 us
  transfers between devices with their start and end apart: 9 -> 21, of which waited for: 8 -> 12; matrix products, arithmetic and copies ran while one was open for 43% -> 37% of each run, Pallas kernels for 0% -> 0%
where the time goes in v1:
time: 396 us; the launch traced here: 391 us
  waiting for transfers between devices  180 us (45%)
  local copies, waits for them, and re-layouts  74.1 us (19%)
  matrix products  63.1 us (16%)
  starting transfers between devices  38.9 us (10%)
  other arithmetic  20.1 us (5%)
  between operations  15.1 us (4%)
    ppermute x14, waiting for transfers between devices, update_cube(): lax.ppermute(part_now, chip_axis, [(at, at ^ d) for at in range(reached)])  96.5 us
    all_to_all x2, waiting for transfers between devices, on_device(): lax.all_to_all(packed[j], 'seq', split_axis=1, concat_axis=1, tiled=True)  53 us
    all_to_all x1, waiting for transfers between devices, on_device(): lax.all_to_all(jnp.stack(col_back, axis=1), 'seq', split_axis=0, concat_a...  24.1 us
    unnamed x126, local copies, waits for them, and re-layouts  24.1 us
    ppermute x14, starting transfers between devices, update_cube(): lax.ppermute(part_now, chip_axis, [(at, at ^ d) for at in range(reached)])  14.5 us
    all_to_all x2, starting transfers between devices, on_device(): lax.all_to_all(packed[j], 'seq', split_axis=1, concat_axis=1, tiled=True)  11.1 us
    dot_general x1, matrix products, on_device(): jnp.dot(attention, weight, preferred_element_type=jnp.float32)  9.7 us
    another operation x8, local copies, waits for them, and re-layouts, on_device(): jnp.stack([g.reshape(rows, piece, half) for g in col_grads])  9.27 us
  transfers between devices with their start and end apart: 21, of which 12 were waited for; matrix products, arithmetic and copies ran while one was open for 37% of the time, Pallas kernels for 0%

profile of v1, /device:TPU:0, one launch (start us, length us, event | category | flops | bytes accessed | tf_op | source)
XLA Modules:
  0.0 391.3 jit_solution(4649671380392426734)
XLA Ops:
  16.5 6.3 %all-to-all-start.1 = ((bf16[3,8,32,1024]{3,2,0,1:T(8,128)(2,1)}), bf16[3,8,32,1024]{3,2,0,1:T(8,128)(2,1)}, u32[]{:S(2)}, u32[]{:S(2)}) async-start(bf16[3,8,32,1024]{3,2,0,1:T(8,128)(2,1)} %copy.216), calls=%async_computation.1 | async-start | bytes 3145728 | tf_op jit(solution)/shard_map/all_to_all | solution.py:105
  31.4 29.3 %all-to-all-done.1 = bf16[3,8,32,1024]{3,2,0,1:T(8,128)(2,1)} async-done(((bf16[3,8,32,1024]{3,2,0,1:T(8,128)(2,1)}), bf16[3,8,32,1024]{3,2,0,1:T(8,128)(2,1)}, u32[]{:S(2)}, u32[]{:S(2)}) %all-to-all-start.1) | async-done | bytes 1572896 | tf_op jit(solution)/shard_map/all_to_all | solution.py:105
  60.7 4.8 %all-to-all-start = ((bf16[3,8,32,1024]{3,2,0,1:T(8,128)(2,1)}), bf16[3,8,32,1024]{3,2,0,1:T(8,128)(2,1)}, u32[]{:S(2)}, u32[]{:S(2)}) async-start(bf16[3,8,32,1024]{3,2,0,1:T(8,128)(2,1)} %copy.208), calls=%async_computation | async-start | bytes 3145728 | tf_op jit(solution)/shard_map/all_to_all | solution.py:105
  79.6 23.7 %all-to-all-done = bf16[3,8,32,1024]{3,2,0,1:T(8,128)(2,1)} async-done(((bf16[3,8,32,1024]{3,2,0,1:T(8,128)(2,1)}), bf16[3,8,32,1024]{3,2,0,1:T(8,128)(2,1)}, u32[]{:S(2)}, u32[]{:S(2)}) %all-to-all-start) | async-done | bytes 1572896 | tf_op jit(solution)/shard_map/all_to_all | solution.py:105
  122.2 4.2 %all-to-all-start.2 = ((bf16[8,2,32,1024]{3,2,1,0:T(8,128)(2,1)}), bf16[8,2,32,1024]{3,2,1,0:T(8,128)(2,1)}, u32[]{:S(2)}, u32[]{:S(2)}) async-start(bf16[8,2,32,1024]{3,2,1,0:T(8,128)(2,1)} %copy.222), calls=%async_computation.2 | async-start | bytes 2097152 | tf_op jit(solution)/shard_map/all_to_all | solution.py:129
  128.9 24.1 %all-to-all-done.2 = bf16[8,2,32,1024]{3,2,1,0:T(8,128)(2,1)} async-done(((bf16[8,2,32,1024]{3,2,1,0:T(8,128)(2,1)}), bf16[8,2,32,1024]{3,2,1,0:T(8,128)(2,1)}, u32[]{:S(2)}, u32[]{:S(2)}) %all-to-all-start.2) | async-done | bytes 1048608 | tf_op jit(solution)/shard_map/all_to_all | solution.py:129
  155.3 8.3 %fusion.14 = bf16[2048,2048]{1,0:T(8,128)(2,1)} fusion(bf16[1,1,512,2048]{3,2,1,0:T(8,128)(2,1)S(1)} %copy-done, bf16[512,1024]{0,1:T(8,128)(2,1)} %copy.223, bf16[512,1024]{0,1:T(8,128)(2,1)} %bitcast.297), kind=kOutput, calls=%fused_computation.31 | convolution fusion | flops 4299161600 | bytes 12582912 | tf_op jit(solution)/shard_map/dot_general | solution.py:133
  166.0 4.5 %fusion.31 = bf16[64,8,8,128]{3,1,2,0:T(8,128)(2,1)S(1)} fusion(bf16[2048,2048]{1,0:T(8,128)(2,1)} %all-gather.2.cloned.1.call-done, bf16[1,1,512,2048]{3,2,1,0:T(8,128)(2,1)S(1)} %copy-done), kind=kOutput, calls=%fused_computation.47 | convolution fusion | flops 2148007936 | bytes 7340032 | tf_op jit(solution)/shard_map/dot_general | solution.py:135
  174.3 4.6 %fusion.18 = bf16[1024,512]{0,1:T(8,128)(2,1)S(1)} fusion(bf16[1,1,512,2048]{3,2,1,0:T(8,128)(2,1)S(1)} %copy-done, bf16[2048,2048]{1,0:T(8,128)(2,1)} %all-gather.2.cloned.1.call-done), kind=kOutput, calls=%fused_computation.44 | convolution fusion | flops 2148007936 | bytes 7340032 | tf_op jit(solution)/shard_map/dot_general | solution.py:139
  188.3 9.2 %collective-permute-done.1 = bf16[1,32,1024]{2,1,0:T(8,128)(2,1)S(1)} collective-permute-done((bf16[1,32,1024]{2,1,0:T(8,128)(2,1)S(1)}, bf16[1,32,1024]{2,1,0:T(8,128)(2,1)S(1)}, u32[]{:S(2)}, u32[]{:S(2)}) %collective-permute-start.1) | collective-permute-done | bytes 65568 | tf_op jit(solution)/shard_map/ppermute | solution.py:158
  199.8 4.9 %collective-permute-done.2 = bf16[1,32,1024]{2,1,0:T(8,128)(2,1)S(1)} collective-permute-done((bf16[1,32,1024]{2,1,0:T(8,128)(2,1)S(1)}, bf16[1,32,1024]{2,1,0:T(8,128)(2,1)S(1)}, u32[]{:S(2)}, u32[]{:S(2)}) %collective-permute-start.2) | collective-permute-done | bytes 65568 | tf_op jit(solution)/shard_map/ppermute | solution.py:158
  205.6 7.7 %collective-permute-done.3 = bf16[1,32,1024]{2,1,0:T(8,128)(2,1)S(1)} collective-permute-done((bf16[1,32,1024]{2,1,0:T(8,128)(2,1)S(1)}, bf16[1,32,1024]{2,1,0:T(8,128)(2,1)S(1)}, u32[]{:S(2)}, u32[]{:S(2)}) %collective-permute-start.3) | collective-permute-done | bytes 65568 | tf_op jit(solution)/shard_map/ppermute | solution.py:158
  213.4 8.2 %collective-permute-done.4 = bf16[1,32,1024]{2,1,0:T(8,128)(2,1)S(1)} collective-permute-done((bf16[1,32,1024]{2,1,0:T(8,128)(2,1)S(1)}, bf16[1,32,1024]{2,1,0:T(8,128)(2,1)S(1)}, u32[]{:S(2)}, u32[]{:S(2)}) %collective-permute-start.4) | collective-permute-done | bytes 65568 | tf_op jit(solution)/shard_map/ppermute | solution.py:158
  222.9 6.0 %collective-permute-done.5 = bf16[1,32,1024]{2,1,0:T(8,128)(2,1)S(1)} collective-permute-done((bf16[1,32,1024]{2,1,0:T(8,128)(2,1)S(1)}, bf16[1,32,1024]{2,1,0:T(8,128)(2,1)S(1)}, u32[]{:S(2)}, u32[]{:S(2)}) %collective-permute-start.5) | collective-permute-done | bytes 65568 | tf_op jit(solution)/shard_map/ppermute | solution.py:158
  229.2 7.2 %collective-permute-done.6 = bf16[1,32,1024]{2,1,0:T(8,128)(2,1)S(1)} collective-permute-done((bf16[1,32,1024]{2,1,0:T(8,128)(2,1)S(1)}, bf16[1,32,1024]{2,1,0:T(8,128)(2,1)S(1)}, u32[]{:S(2)}, u32[]{:S(2)}) %collective-permute-start.6) | collective-permute-done | bytes 65568 | tf_op jit(solution)/shard_map/ppermute | solution.py:158
  250.7 3.9 %all-to-all-start.3 = ((bf16[3,8,32,1024]{3,2,0,1:T(8,128)(2,1)}), bf16[3,8,32,1024]{3,2,0,1:T(8,128)(2,1)S(1)}, u32[]{:S(2)}, u32[]{:S(2)}) async-start(bf16[3,8,32,1024]{3,2,0,1:T(8,128)(2,1)} %copy.238), calls=%async_computation.3 | async-start | bytes 3145728 | tf_op jit(solution)/shard_map/all_to_all | solution.py:172
  257.5 46.8 %collective-permute-done.8 = bf16[1,32,1024]{2,1,0:T(8,128)(2,1)S(1)} collective-permute-done((bf16[1,32,1024]{2,1,0:T(8,128)(2,1)}, bf16[1,32,1024]{2,1,0:T(8,128)(2,1)S(1)}, u32[]{:S(2)}, u32[]{:S(2)}) %collective-permute-start.8) | collective-permute-done | bytes 65568 | tf_op jit(solution)/shard_map/ppermute | solution.py:158
  305.8 6.5 %collective-permute-done.9 = bf16[1,32,1024]{2,1,0:T(8,128)(2,1)S(1)} collective-permute-done((bf16[1,32,1024]{2,1,0:T(8,128)(2,1)}, bf16[1,32,1024]{2,1,0:T(8,128)(2,1)S(1)}, u32[]{:S(2)}, u32[]{:S(2)}) %collective-permute-start.9) | collective-permute-done | bytes 65568 | tf_op jit(solution)/shard_map/ppermute | solution.py:158
  332.2 4.9 %all-to-all-start.4 = ((bf16[3,8,32,1024]{3,2,0,1:T(8,128)(2,1)}), bf16[3,8,32,1024]{3,2,0,1:T(8,128)(2,1)}, u32[]{:S(2)}, u32[]{:S(2)}) async-start(bf16[3,8,32,1024]{3,2,0,1:T(8,128)(2,1)} %copy.250), calls=%async_computation.4 | async-start | bytes 3145728 | tf_op jit(solution)/shard_map/all_to_all | solution.py:172
  337.2 5.5 %multiply_convert_fusion = bf16[8,512,512]{1,2,0:T(8,128)(2,1)S(1)} fusion(f32[8,512,512]{1,2,0:T(8,128)} %copy-done.2, f32[8,512]{1,0:T(8,128)S(1)} %multiply_reduce_fusion, f32[8,512]{1,0:T(8,128)S(1)} %bitcast.304, pred[512,512]{0,1:T(8,128)(4,1)S(1)} %fusion.53, bf16[512,8,128]{0,2,1:T(8,128)(2,1)} %copy.255, bf16[512,8,128]{0,2,1:T(8,128)(2,1)S(1)} %bitcast.269), kind=kOutput, calls=%fused_computation.2 | convolution fusion | flops 547356672 | bytes 14974976 | tf_op jit(solution)/shard_map/ihd,jhd->hij/dot_general | solution.py:58
  346.1 3.8 multiply_convert_fusion.1
  351.2 6.1 %fusion.28 = bf16[8,128,512]{2,1,0:T(8,128)(2,1)} fusion(bf16[512,8,128]{0,2,1:T(8,128)(2,1)S(1)} %copy-done.18, f32[8,512,512]{1,2,0:T(8,128)} %copy-done.2, f32[8,512]{1,0:T(8,128)S(1)} %bitcast.305, pred[512,512]{0,1:T(8,128)(4,1)S(1)} %fusion.53), kind=kOutput, calls=%fused_computation.46 | convolution fusion | flops 543686656 | bytes 10764288 | tf_op jit(solution)/shard_map/hij,ihd->jhd/dot_general | solution.py:55
  359.5 9.7 %fusion.12 = bf16[1,1,512,2048]{3,2,1,0:T(8,128)(2,1)} fusion(bf16[2048,2048]{1,0:T(8,128)(2,1)} %all-gather.2.cloned.1.call-done, bf16[512,1024]{0,1:T(8,128)(2,1)} %copy.223, bf16[512,1024]{0,1:T(8,128)(2,1)S(1)} %bitcast.298), kind=kOutput, calls=%fused_computation.25 | convolution fusion | flops 4300210176 | bytes 12582912 | tf_op jit(solution)/shard_map/dot_general | solution.py:191
  369.4 5.6 %all-to-all-done.4 = bf16[3,8,32,1024]{3,2,0,1:T(8,128)(2,1)} async-done(((bf16[3,8,32,1024]{3,2,0,1:T(8,128)(2,1)}), bf16[3,8,32,1024]{3,2,0,1:T(8,128)(2,1)}, u32[]{:S(2)}, u32[]{:S(2)}) %all-to-all-start.4) | async-done | bytes 1572896 | tf_op jit(solution)/shard_map/all_to_all | solution.py:172
  (236 shorter events, 130.3 us)
Async XLA Ops:
  7.2 148.1 %copy-start = (bf16[1,1,512,2048]{3,2,1,0:T(8,128)(2,1)S(1)}, bf16[1,1,512,2048]{3,2,1,0:T(8,128)(2,1)}, u32[]{:S(2)}) copy-start(bf16[1,1,512,2048]{3,2,1,0:T(8,128)(2,1)} %param.10) | copy-start | bytes 6291460
  7.2 156.4 %all-gather.2.cloned.1.call-start = ((), (), s32[]{:S(2)}) async-start(), calls=%async_computation.6 | async-start | bytes 10485760 | tf_op jit(solution)/shard_map/all_gather | solution.py:95
  16.5 44.3 %all-to-all-start.1 = ((bf16[3,8,32,1024]{3,2,0,1:T(8,128)(2,1)}), bf16[3,8,32,1024]{3,2,0,1:T(8,128)(2,1)}, u32[]{:S(2)}, u32[]{:S(2)}) async-start(bf16[3,8,32,1024]{3,2,0,1:T(8,128)(2,1)} %copy.216), calls=%async_computation.1 | async-start | bytes 3145728 | tf_op jit(solution)/shard_map/all_to_all | solution.py:105
  23.0 90.9 %copy-start.45 = (pred[8,8]{0,1:T(8,128)(4,1)}, pred[8,8]{0,1:T(8,128)(4,1)S(1)}, u32[]{:S(2)}) copy-start(pred[8,8]{0,1:T(8,128)(4,1)S(1)} %copy.210) | copy-start | bytes 196
  60.7 42.6 %all-to-all-start = ((bf16[3,8,32,1024]{3,2,0,1:T(8,128)(2,1)}), bf16[3,8,32,1024]{3,2,0,1:T(8,128)(2,1)}, u32[]{:S(2)}, u32[]{:S(2)}) async-start(bf16[3,8,32,1024]{3,2,0,1:T(8,128)(2,1)} %copy.208), calls=%async_computation | async-start | bytes 3145728 | tf_op jit(solution)/shard_map/all_to_all | solution.py:105
  122.2 30.8 %all-to-all-start.2 = ((bf16[8,2,32,1024]{3,2,1,0:T(8,128)(2,1)}), bf16[8,2,32,1024]{3,2,1,0:T(8,128)(2,1)}, u32[]{:S(2)}, u32[]{:S(2)}) async-start(bf16[8,2,32,1024]{3,2,1,0:T(8,128)(2,1)} %copy.222), calls=%async_computation.2 | async-start | bytes 2097152 | tf_op jit(solution)/shard_map/all_to_all | solution.py:129
  126.4 256.0 %reduce-scatter.2.cloned.1.call-start = ((), (), s32[]{:S(2)}) async-start(), calls=%async_computation.7 | async-start | bytes 8650752 | tf_op jit(solution)/shard_map/reduce_scatter | solution.py:144
  179.0 9.2 %collective-permute-start = (bf16[1,32,1024]{2,1,0:T(8,128)(2,1)S(1)}, bf16[1,32,1024]{2,1,0:T(8,128)(2,1)S(1)}, u32[]{:S(2)}, u32[]{:S(2)}) collective-permute-start(bf16[1,32,1024]{2,1,0:T(8,128)(2,1)S(1)} %get-tuple-element.52), channel_id=1, source_target_pairs={{0,1},{1,0},{2,3},{3,2},{4,5},{5,4},{6,7},{7,6},{8,9},{9,8},{10,11... | collective-permute-start | bytes 196616 | tf_op jit(solution)/shard_map/ppermute | solution.py:158
  180.4 58.6 %copy-start.6 = (f32[32,8,8,8]{2,3,1,0:T(8,128)S(1)}, f32[32,8,8,8]{2,3,1,0:T(8,128)}, u32[]{:S(2)}) copy-start(f32[32,8,8,8]{2,3,1,0:T(8,128)} %copy-done.5) | copy-start | bytes 196612
  182.1 132.7 %collective-permute-start.13 = (bf16[1,32,1024]{2,1,0:T(8,128)(2,1)}, bf16[1,32,1024]{2,1,0:T(8,128)(2,1)}, u32[]{:S(2)}, u32[]{:S(2)}) collective-permute-start(bf16[1,32,1024]{2,1,0:T(8,128)(2,1)} %get-tuple-element.38), channel_id=1, source_target_pairs={{0,7},{1,6},{2,5},{3,4},{4,3},{5,2},{6,1},{7,0},{8,15},{9,14},{10,... | collective-permute-start | bytes 196616 | tf_op jit(solution)/shard_map/ppermute | solution.py:158
  183.0 130.9 %collective-permute-start.12 = (bf16[1,32,1024]{2,1,0:T(8,128)(2,1)}, bf16[1,32,1024]{2,1,0:T(8,128)(2,1)}, u32[]{:S(2)}, u32[]{:S(2)}) collective-permute-start(bf16[1,32,1024]{2,1,0:T(8,128)(2,1)} %get-tuple-element.39), channel_id=1, source_target_pairs={{0,6},{1,7},{2,4},{3,5},{4,2},{5,3},{6,0},{7,1},{8,14},{9,15},{10,... | collective-permute-start | bytes 196616 | tf_op jit(solution)/shard_map/ppermute | solution.py:158
  185.1 128.0 %collective-permute-start.11 = (bf16[1,32,1024]{2,1,0:T(8,128)(2,1)}, bf16[1,32,1024]{2,1,0:T(8,128)(2,1)}, u32[]{:S(2)}, u32[]{:S(2)}) collective-permute-start(bf16[1,32,1024]{2,1,0:T(8,128)(2,1)} %get-tuple-element.40), channel_id=1, source_target_pairs={{0,5},{1,4},{2,7},{3,6},{4,1},{5,0},{6,3},{7,2},{8,13},{9,12},{10,... | collective-permute-start | bytes 196616 | tf_op jit(solution)/shard_map/ppermute | solution.py:158
  185.1 127.1 %collective-permute-start.10 = (bf16[1,32,1024]{2,1,0:T(8,128)(2,1)}, bf16[1,32,1024]{2,1,0:T(8,128)(2,1)}, u32[]{:S(2)}, u32[]{:S(2)}) collective-permute-start(bf16[1,32,1024]{2,1,0:T(8,128)(2,1)} %get-tuple-element.41), channel_id=1, source_target_pairs={{0,4},{1,5},{2,6},{3,7},{4,0},{5,1},{6,2},{7,3},{8,12},{9,13},{10,... | collective-permute-start | bytes 196616 | tf_op jit(solution)/shard_map/ppermute | solution.py:158
  188.3 9.3 %collective-permute-start.1 = (bf16[1,32,1024]{2,1,0:T(8,128)(2,1)S(1)}, bf16[1,32,1024]{2,1,0:T(8,128)(2,1)S(1)}, u32[]{:S(2)}, u32[]{:S(2)}) collective-permute-start(bf16[1,32,1024]{2,1,0:T(8,128)(2,1)S(1)} %get-tuple-element.51), channel_id=1, source_target_pairs={{0,2},{1,3},{2,0},{3,1},{4,6},{5,7},{6,4},{7,5},{8,10},{9,11},{10,... | collective-permute-start | bytes 196616 | tf_op jit(solution)/shard_map/ppermute | solution.py:158
  197.5 7.2 %collective-permute-start.2 = (bf16[1,32,1024]{2,1,0:T(8,128)(2,1)S(1)}, bf16[1,32,1024]{2,1,0:T(8,128)(2,1)S(1)}, u32[]{:S(2)}, u32[]{:S(2)}) collective-permute-start(bf16[1,32,1024]{2,1,0:T(8,128)(2,1)S(1)} %get-tuple-element.50), channel_id=1, source_target_pairs={{0,3},{1,2},{2,1},{3,0},{4,7},{5,6},{6,5},{7,4},{8,11},{9,10},{10,... | collective-permute-start | bytes 196616 | tf_op jit(solution)/shard_map/ppermute | solution.py:158
  204.7 8.6 %collective-permute-start.3 = (bf16[1,32,1024]{2,1,0:T(8,128)(2,1)S(1)}, bf16[1,32,1024]{2,1,0:T(8,128)(2,1)S(1)}, u32[]{:S(2)}, u32[]{:S(2)}) collective-permute-start(bf16[1,32,1024]{2,1,0:T(8,128)(2,1)S(1)} %get-tuple-element.49), channel_id=1, source_target_pairs={{0,4},{1,5},{2,6},{3,7},{4,0},{5,1},{6,2},{7,3},{8,12},{9,13},{10,... | collective-permute-start | bytes 196616 | tf_op jit(solution)/shard_map/ppermute | solution.py:158
  213.4 8.2 %collective-permute-start.4 = (bf16[1,32,1024]{2,1,0:T(8,128)(2,1)S(1)}, bf16[1,32,1024]{2,1,0:T(8,128)(2,1)S(1)}, u32[]{:S(2)}, u32[]{:S(2)}) collective-permute-start(bf16[1,32,1024]{2,1,0:T(8,128)(2,1)S(1)} %get-tuple-element.48), channel_id=1, source_target_pairs={{0,5},{1,4},{2,7},{3,6},{4,1},{5,0},{6,3},{7,2},{8,13},{9,12},{10,... | collective-permute-start | bytes 196616 | tf_op jit(solution)/shard_map/ppermute | solution.py:158
  221.6 7.4 %collective-permute-start.5 = (bf16[1,32,1024]{2,1,0:T(8,128)(2,1)S(1)}, bf16[1,32,1024]{2,1,0:T(8,128)(2,1)S(1)}, u32[]{:S(2)}, u32[]{:S(2)}) collective-permute-start(bf16[1,32,1024]{2,1,0:T(8,128)(2,1)S(1)} %get-tuple-element.47), channel_id=1, source_target_pairs={{0,6},{1,7},{2,4},{3,5},{4,2},{5,3},{6,0},{7,1},{8,14},{9,15},{10,... | collective-permute-start | bytes 196616 | tf_op jit(solution)/shard_map/ppermute | solution.py:158
  229.0 7.4 %collective-permute-start.6 = (bf16[1,32,1024]{2,1,0:T(8,128)(2,1)S(1)}, bf16[1,32,1024]{2,1,0:T(8,128)(2,1)S(1)}, u32[]{:S(2)}, u32[]{:S(2)}) collective-permute-start(bf16[1,32,1024]{2,1,0:T(8,128)(2,1)S(1)} %get-tuple-element.46), channel_id=1, source_target_pairs={{0,7},{1,6},{2,5},{3,4},{4,3},{5,2},{6,1},{7,0},{8,15},{9,14},{10,... | collective-permute-start | bytes 196616 | tf_op jit(solution)/shard_map/ppermute | solution.py:158
  236.3 18.3 %collective-permute-start.7 = (bf16[1,32,1024]{2,1,0:T(8,128)(2,1)}, bf16[1,32,1024]{2,1,0:T(8,128)(2,1)}, u32[]{:S(2)}, u32[]{:S(2)}) collective-permute-start(bf16[1,32,1024]{2,1,0:T(8,128)(2,1)} %get-tuple-element.44), channel_id=1, source_target_pairs={{0,1},{1,0},{2,3},{3,2},{4,5},{5,4},{6,7},{7,6},{8,9},{9,8},{10,11... | collective-permute-start | bytes 196616 | tf_op jit(solution)/shard_map/ppermute | solution.py:158
  250.7 81.5 %all-to-all-start.3 = ((bf16[3,8,32,1024]{3,2,0,1:T(8,128)(2,1)}), bf16[3,8,32,1024]{3,2,0,1:T(8,128)(2,1)S(1)}, u32[]{:S(2)}, u32[]{:S(2)}) async-start(bf16[3,8,32,1024]{3,2,0,1:T(8,128)(2,1)} %copy.238), calls=%async_computation.3 | async-start | bytes 3145728 | tf_op jit(solution)/shard_map/all_to_all | solution.py:172
  254.6 49.6 %collective-permute-start.8 = (bf16[1,32,1024]{2,1,0:T(8,128)(2,1)}, bf16[1,32,1024]{2,1,0:T(8,128)(2,1)S(1)}, u32[]{:S(2)}, u32[]{:S(2)}) collective-permute-start(bf16[1,32,1024]{2,1,0:T(8,128)(2,1)} %get-tuple-element.43), channel_id=1, source_target_pairs={{0,2},{1,3},{2,0},{3,1},{4,6},{5,7},{6,4},{7,5},{8,10},{9,11},{10,... | collective-permute-start | bytes 196616 | tf_op jit(solution)/shard_map/ppermute | solution.py:158
  304.3 8.0 %collective-permute-start.9 = (bf16[1,32,1024]{2,1,0:T(8,128)(2,1)}, bf16[1,32,1024]{2,1,0:T(8,128)(2,1)S(1)}, u32[]{:S(2)}, u32[]{:S(2)}) collective-permute-start(bf16[1,32,1024]{2,1,0:T(8,128)(2,1)} %get-tuple-element.42), channel_id=1, source_target_pairs={{0,3},{1,2},{2,1},{3,0},{4,7},{5,6},{6,5},{7,4},{8,11},{9,10},{10,... | collective-permute-start | bytes 196616 | tf_op jit(solution)/shard_map/ppermute | solution.py:158
  332.2 42.8 %all-to-all-start.4 = ((bf16[3,8,32,1024]{3,2,0,1:T(8,128)(2,1)}), bf16[3,8,32,1024]{3,2,0,1:T(8,128)(2,1)}, u32[]{:S(2)}, u32[]{:S(2)}) async-start(bf16[3,8,32,1024]{3,2,0,1:T(8,128)(2,1)} %copy.250), calls=%async_computation.4 | async-start | bytes 3145728 | tf_op jit(solution)/shard_map/all_to_all | solution.py:172
  (47 other events, 183.5 us)
Sparse Core Ops, SparseCore 0:
  9.9 90.2 all-gather.1
  163.7 168.3 reduce-scatter.1
